TPU v7x, 32 devices: a whole 2x2x4 slice. The times are simulated.
32 devices in a mesh: gx: 8 (over z, x), gy: 4 (over y, core).
Axes of the slice: x: 2, y: 2, z: 4, core: 2. Of those that a mesh axis runs over, the one named last changes fastest.
Arguments:
- fields: bfloat16 [4, 64, 128, 256], P(None, 'gx', 'gy'), may hold values from -6 to 6
- rows_live: int32 [8], replicated, may hold values from 4 to 8, as said below
- cols_live: int32 [4], replicated, may hold values from 16 to 32, as said below
- weight: bfloat16 [32, 108], replicated, may hold values from -0.625 to 0.625
- bias: float32 [32], replicated, may hold values from -3 to 3
- grad_out: bfloat16 [32, 32, 64, 128], P('gy', 'gx'), may hold values from -0.0625 to 0.0625
Outputs:
- stem: bfloat16 [32, 32, 64, 128], P('gy', 'gx')
- weight_grad: float32 [32, 108], P('gy')
- bias_grad: float32 [32], P('gy')
Inputs may be any that keep to these rules, and one draw needn't show every extreme that they name: `rows_live`: every entry is even, and some entry equals 8. `cols_live`: every entry is even, and some entry equals 32.
All inputs are finite; a program needn't handle non-finite values.
Results may differ from a plain program's by a relative error of at most 0.0054.
Values may be sent and summed in bfloat16 or wider, within the bound.
No kernel may reach another device: no remote copies, remote signals or barrier semaphores. Data moves between devices by JAX's collectives and lax.ppermute only.
A program may use at most 64 MiB of HBM per device.

v0:
```python
import jax
import jax.numpy as jnp
from jax import lax
from jax.sharding import PartitionSpec as P


def from_behind(block, axis, distance):
    devices = range(lax.axis_size(axis))
    route = [(i - distance, i) for i in devices if i - distance in devices]
    return lax.ppermute(block, axis, route)


def extend(data, border, count, dim):
    length = data.shape[dim]
    border_wide = jnp.expand_dims(border, dim)
    joined = jnp.concatenate([jnp.zeros_like(border_wide), data], axis=dim)
    shape = [1] * joined.ndim
    shape[dim] = length + 1
    places = jnp.arange(length + 1, dtype=jnp.int32).reshape(shape)
    edge_at = length - count
    kept = jnp.where(places > edge_at, joined, jnp.zeros_like(joined))
    return jnp.where(places == edge_at, border_wide, kept)


def taps(padded, axes, halves):
    pieces = []
    for off_x in range(3):
        for off_y in range(3):
            for off_z in range(3):
                piece = padded
                for axis_no, offset, half in zip(axes, (off_x, off_y, off_z), halves):
                    piece = lax.slice_in_dim(piece, offset, offset + 2 * half - 1, 2, axis_no)
                pieces.append(piece)
    return pieces


def local(fields, rows_live, cols_live, weight, bias, grad_out):
    in_chans, cap_x, cap_y, depth = fields.shape
    half_x = cap_x // 2
    half_y = cap_y // 2
    half_z = depth // 2
    out_chans = weight.shape[0]
    tiles_y = lax.axis_size("gy")
    row_count = rows_live[lax.axis_index("gx")]
    above = from_behind(fields[:, cap_x - 1], "gx", 1)
    ext_rows = extend(fields, above, row_count, 1)
    row_ok = jnp.arange(half_x, dtype=jnp.int32) >= half_x - row_count // 2
    col_count = cols_live[lax.axis_index("gy")]
    beside = from_behind(ext_rows[:, :, cap_y - 1], "gy", 1)
    ext_full = extend(ext_rows, beside, col_count, 2)
    padded = jnp.pad(ext_full, ((0, 0), (0, 0), (0, 0), (1, 0)))
    patches = jnp.stack(taps(padded, (1, 2, 3), (half_x, half_y, half_z)), axis=1).reshape(
        in_chans * 27, -1
    )
    conv = jnp.dot(weight, patches, preferred_element_type=jnp.float32) + bias[:, None]
    col_ok = jnp.arange(half_y, dtype=jnp.int32) >= half_y - col_count // 2
    live = (row_ok[:, None] & col_ok[None, :]).reshape(1, half_x, half_y, 1)
    conv = conv.reshape(out_chans, half_x, half_y, half_z)
    pre_local = jnp.where(live, conv, 0.0).astype(jnp.bfloat16)
    regrouped = lax.all_to_all(pre_local, "gy", split_axis=0, concat_axis=2, tiled=True)
    pre_wide = regrouped.astype(jnp.float32)
    sigma = jax.nn.sigmoid(pre_wide)
    stem = (pre_wide * sigma).astype(jnp.bfloat16)
    wide_cols = jnp.arange(half_y, dtype=jnp.int32)[None, :] >= half_y - (cols_live // 2)[:, None]
    wide_live = row_ok.reshape(1, half_x, 1, 1) & wide_cols.reshape(1, 1, tiles_y * half_y, 1)
    slope = sigma * (1.0 + pre_wide * (1.0 - sigma))
    grad_pre = jnp.where(wide_live, grad_out.astype(jnp.float32) * slope, 0.0).astype(jnp.bfloat16)
    returned = lax.all_to_all(grad_pre, "gy", split_axis=2, concat_axis=0, tiled=True)
    flat = returned.reshape(out_chans, -1)
    weight_full = lax.dot_general(
        flat, patches, (((1,), (1,)), ((), ())), preferred_element_type=jnp.float32
    )
    bias_full = jnp.sum(flat.astype(jnp.float32), axis=1)
    weight_part, bias_part = (
        lax.psum_scatter(weight_full, "gy", scatter_dimension=0, tiled=True),
        lax.psum_scatter(bias_full, "gy", scatter_dimension=0, tiled=True),
    )
    weight_grad, bias_grad = lax.psum((weight_part, bias_part), "gx")
    return (stem, weight_grad, bias_grad)


def solution(mesh):
    in_specs = (P(None, "gx", "gy", None), P(), P(), P(), P(), P("gy", "gx", None, None))
    out_specs = (P("gy", "gx", None, None), P("gy", None), P("gy"))
    return jax.shard_map(local, mesh=mesh, in_specs=in_specs, out_specs=out_specs, check_vma=False)
```

profile of v0, /device:TPU:0, one launch (start us, length us, event | category | flops | bytes accessed | tf_op | source)
XLA Modules:
  0.0 160.4 jit_solution(18269219123622887395)
XLA Ops:
  1.5 4.9 %collective-permute-start = (bf16[4,32,256]{2,1,0:T(8,128)(2,1)S(1)}, bf16[4,32,256]{2,1,0:T(8,128)(2,1)S(1)}, u32[]{:S(2)}, u32[]{:S(2)}) collective-permute-start(bf16[4,32,256]{2,1,0:T(8,128)(2,1)S(1)} %slice_bitcast_fusion), channel_id=1, source_target_pairs={{0,4},{4,8},{8,12},{12,16},{16,20},{20,24},{24,28},{1,5},{5,9},{9,... | collective-permute-start | bytes 196616 | tf_op jit(solution)/shard_map/ppermute | solution.py:10
  21.1 2.5 %slice.205 = bf16[4,4,16,128]{3,2,1,0:T(8,128)(2,1)S(1)} slice(bf16[4,4,16,257]{3,2,1,0:T(8,128)(2,1)S(1)} %slice.202), slice={[0:4:1], [0:4:1], [0:16:1], [2:257:2]} | slice | bytes 131072 | tf_op jit(solution)/shard_map/slice | solution.py:32
  23.7 2.5 %slice.204 = bf16[4,4,16,128]{3,2,1,0:T(8,128)(2,1)S(1)} slice(bf16[4,4,16,257]{3,2,1,0:T(8,128)(2,1)S(1)} %slice.202), slice={[0:4:1], [0:4:1], [0:16:1], [1:256:2]} | slice | bytes 131072 | tf_op jit(solution)/shard_map/slice | solution.py:32
  26.2 2.5 %slice.203 = bf16[4,4,16,128]{3,2,1,0:T(8,128)(2,1)S(1)} slice(bf16[4,4,16,257]{3,2,1,0:T(8,128)(2,1)S(1)} %slice.202), slice={[0:4:1], [0:4:1], [0:16:1], [0:255:2]} | slice | bytes 131072 | tf_op jit(solution)/shard_map/slice | solution.py:32
  29.4 2.5 %slice.197 = bf16[4,4,16,128]{3,2,1,0:T(8,128)(2,1)S(1)} slice(bf16[4,4,16,257]{3,2,1,0:T(8,128)(2,1)S(1)} %slice.194), slice={[0:4:1], [0:4:1], [0:16:1], [2:257:2]} | slice | bytes 131072 | tf_op jit(solution)/shard_map/slice | solution.py:32
  31.9 2.5 %slice.196 = bf16[4,4,16,128]{3,2,1,0:T(8,128)(2,1)S(1)} slice(bf16[4,4,16,257]{3,2,1,0:T(8,128)(2,1)S(1)} %slice.194), slice={[0:4:1], [0:4:1], [0:16:1], [1:256:2]} | slice | bytes 131072 | tf_op jit(solution)/shard_map/slice | solution.py:32
  34.5 2.5 %slice.195 = bf16[4,4,16,128]{3,2,1,0:T(8,128)(2,1)S(1)} slice(bf16[4,4,16,257]{3,2,1,0:T(8,128)(2,1)S(1)} %slice.194), slice={[0:4:1], [0:4:1], [0:16:1], [0:255:2]} | slice | bytes 131072 | tf_op jit(solution)/shard_map/slice | solution.py:32
  37.0 2.5 %slice.201 = bf16[4,4,16,128]{3,2,1,0:T(8,128)(2,1)S(1)} slice(bf16[4,4,16,257]{3,2,1,0:T(8,128)(2,1)S(1)} %slice.198), slice={[0:4:1], [0:4:1], [0:16:1], [2:257:2]} | slice | bytes 131072 | tf_op jit(solution)/shard_map/slice | solution.py:32
  39.6 2.5 %slice.200 = bf16[4,4,16,128]{3,2,1,0:T(8,128)(2,1)S(1)} slice(bf16[4,4,16,257]{3,2,1,0:T(8,128)(2,1)S(1)} %slice.198), slice={[0:4:1], [0:4:1], [0:16:1], [1:256:2]} | slice | bytes 131072 | tf_op jit(solution)/shard_map/slice | solution.py:32
  42.1 2.5 %slice.199 = bf16[4,4,16,128]{3,2,1,0:T(8,128)(2,1)S(1)} slice(bf16[4,4,16,257]{3,2,1,0:T(8,128)(2,1)S(1)} %slice.198), slice={[0:4:1], [0:4:1], [0:16:1], [0:255:2]} | slice | bytes 131072 | tf_op jit(solution)/shard_map/slice | solution.py:32
  45.0 2.5 %slice.192 = bf16[4,4,16,128]{3,2,1,0:T(8,128)(2,1)S(1)} slice(bf16[4,4,16,257]{3,2,1,0:T(8,128)(2,1)S(1)} %slice.189), slice={[0:4:1], [0:4:1], [0:16:1], [2:257:2]} | slice | bytes 131072 | tf_op jit(solution)/shard_map/slice | solution.py:32
  47.5 2.5 %slice.191 = bf16[4,4,16,128]{3,2,1,0:T(8,128)(2,1)S(1)} slice(bf16[4,4,16,257]{3,2,1,0:T(8,128)(2,1)S(1)} %slice.189), slice={[0:4:1], [0:4:1], [0:16:1], [1:256:2]} | slice | bytes 131072 | tf_op jit(solution)/shard_map/slice | solution.py:32
  50.1 2.5 %slice.190 = bf16[4,4,16,128]{3,2,1,0:T(8,128)(2,1)S(1)} slice(bf16[4,4,16,257]{3,2,1,0:T(8,128)(2,1)S(1)} %slice.189), slice={[0:4:1], [0:4:1], [0:16:1], [0:255:2]} | slice | bytes 131072 | tf_op jit(solution)/shard_map/slice | solution.py:32
  53.2 2.5 %slice.184 = bf16[4,4,16,128]{3,2,1,0:T(8,128)(2,1)S(1)} slice(bf16[4,4,16,257]{3,2,1,0:T(8,128)(2,1)S(1)} %slice.181), slice={[0:4:1], [0:4:1], [0:16:1], [2:257:2]} | slice | bytes 131072 | tf_op jit(solution)/shard_map/slice | solution.py:32
  55.8 2.5 %slice.183 = bf16[4,4,16,128]{3,2,1,0:T(8,128)(2,1)S(1)} slice(bf16[4,4,16,257]{3,2,1,0:T(8,128)(2,1)S(1)} %slice.181), slice={[0:4:1], [0:4:1], [0:16:1], [1:256:2]} | slice | bytes 131072 | tf_op jit(solution)/shard_map/slice | solution.py:32
  58.3 2.5 %slice.182 = bf16[4,4,16,128]{3,2,1,0:T(8,128)(2,1)S(1)} slice(bf16[4,4,16,257]{3,2,1,0:T(8,128)(2,1)S(1)} %slice.181), slice={[0:4:1], [0:4:1], [0:16:1], [0:255:2]} | slice | bytes 131072 | tf_op jit(solution)/shard_map/slice | solution.py:32
  60.9 2.5 %slice.188 = bf16[4,4,16,128]{3,2,1,0:T(8,128)(2,1)S(1)} slice(bf16[4,4,16,257]{3,2,1,0:T(8,128)(2,1)S(1)} %slice.185), slice={[0:4:1], [0:4:1], [0:16:1], [2:257:2]} | slice | bytes 131072 | tf_op jit(solution)/shard_map/slice | solution.py:32
  63.4 2.5 %slice.187 = bf16[4,4,16,128]{3,2,1,0:T(8,128)(2,1)S(1)} slice(bf16[4,4,16,257]{3,2,1,0:T(8,128)(2,1)S(1)} %slice.185), slice={[0:4:1], [0:4:1], [0:16:1], [1:256:2]} | slice | bytes 131072 | tf_op jit(solution)/shard_map/slice | solution.py:32
  66.0 2.5 %slice.186 = bf16[4,4,16,128]{3,2,1,0:T(8,128)(2,1)S(1)} slice(bf16[4,4,16,257]{3,2,1,0:T(8,128)(2,1)S(1)} %slice.185), slice={[0:4:1], [0:4:1], [0:16:1], [0:255:2]} | slice | bytes 131072 | tf_op jit(solution)/shard_map/slice | solution.py:32
  68.9 2.5 %slice.179 = bf16[4,4,16,128]{3,2,1,0:T(8,128)(2,1)S(1)} slice(bf16[4,4,16,257]{3,2,1,0:T(8,128)(2,1)S(1)} %slice.176), slice={[0:4:1], [0:4:1], [0:16:1], [2:257:2]} | slice | bytes 131072 | tf_op jit(solution)/shard_map/slice | solution.py:32
  71.4 2.5 %slice.178 = bf16[4,4,16,128]{3,2,1,0:T(8,128)(2,1)S(1)} slice(bf16[4,4,16,257]{3,2,1,0:T(8,128)(2,1)S(1)} %slice.176), slice={[0:4:1], [0:4:1], [0:16:1], [1:256:2]} | slice | bytes 131072 | tf_op jit(solution)/shard_map/slice | solution.py:32
  77.1 2.7 %slice.171 = bf16[4,4,16,128]{3,2,1,0:T(8,128)(2,1)S(1)} slice(bf16[4,4,16,257]{3,2,1,0:T(8,128)(2,1)S(1)} %slice.168), slice={[0:4:1], [0:4:1], [0:16:1], [2:257:2]} | slice | bytes 131072 | tf_op jit(solution)/shard_map/slice | solution.py:32
  79.8 2.5 %slice.170 = bf16[4,4,16,128]{3,2,1,0:T(8,128)(2,1)S(1)} slice(bf16[4,4,16,257]{3,2,1,0:T(8,128)(2,1)S(1)} %slice.168), slice={[0:4:1], [0:4:1], [0:16:1], [1:256:2]} | slice | bytes 131072 | tf_op jit(solution)/shard_map/slice | solution.py:32
  84.9 2.5 %slice.175 = bf16[4,4,16,128]{3,2,1,0:T(8,128)(2,1)S(1)} slice(bf16[4,4,16,257]{3,2,1,0:T(8,128)(2,1)S(1)} %slice.172), slice={[0:4:1], [0:4:1], [0:16:1], [2:257:2]} | slice | bytes 131072 | tf_op jit(solution)/shard_map/slice | solution.py:32
  87.5 2.5 %slice.174 = bf16[4,4,16,128]{3,2,1,0:T(8,128)(2,1)S(1)} slice(bf16[4,4,16,257]{3,2,1,0:T(8,128)(2,1)S(1)} %slice.172), slice={[0:4:1], [0:4:1], [0:16:1], [1:256:2]} | slice | bytes 131072 | tf_op jit(solution)/shard_map/slice | solution.py:32
  94.6 2.7 %reshape.144 = bf16[108,8192]{1,0:T(8,128)(2,1)S(1)} reshape(bf16[4,27,4,16,128]{4,3,2,1,0:T(8,128)(2,1)} %copy.24) | data formatting | bytes 3538944 | tf_op jit(solution)/shard_map/reshape | solution.py:52
  98.9 5.6 %all-to-all-start = ((bf16[32,4,16,128]{3,2,1,0:T(8,128)(2,1)}), bf16[32,4,16,128]{3,2,1,0:T(8,128)(2,1)S(1)}, u32[]{:S(2)}, u32[]{:S(2)}) async-start(bf16[32,4,16,128]{3,2,1,0:T(8,128)(2,1)} %select_convert_fusion), calls=%async_computation | async-start | bytes 1048576 | tf_op jit(solution)/shard_map/all_to_all | solution.py:60
  104.7 8.6 %all-to-all-done = bf16[32,4,16,128]{3,2,1,0:T(8,128)(2,1)S(1)} async-done(((bf16[32,4,16,128]{3,2,1,0:T(8,128)(2,1)}), bf16[32,4,16,128]{3,2,1,0:T(8,128)(2,1)S(1)}, u32[]{:S(2)}, u32[]{:S(2)}) %all-to-all-start) | async-done | bytes 524320 | tf_op jit(solution)/shard_map/all_to_all | solution.py:60
  116.0 3.5 %all-to-all-start.1 = ((bf16[8,4,64,128]{3,0,1,2:T(8,128)(2,1)}), bf16[8,4,64,128]{3,0,1,2:T(8,128)(2,1)S(1)}, u32[]{:S(2)}, u32[]{:S(2)}) async-start(bf16[8,4,64,128]{3,0,1,2:T(8,128)(2,1)} %get-tuple-element.13), calls=%async_computation.1 | async-start | bytes 1048576 | tf_op jit(solution)/shard_map/all_to_all | solution.py:68
  121.7 6.5 %all-to-all-done.1 = bf16[8,4,64,128]{3,0,1,2:T(8,128)(2,1)S(1)} async-done(((bf16[8,4,64,128]{3,0,1,2:T(8,128)(2,1)}), bf16[8,4,64,128]{3,0,1,2:T(8,128)(2,1)S(1)}, u32[]{:S(2)}, u32[]{:S(2)}) %all-to-all-start.1) | async-done | bytes 524320 | tf_op jit(solution)/shard_map/all_to_all | solution.py:68
  129.8 10.3 %all-reduce.6 = (f32[32,108]{1,0:T(8,128)S(1)}, f32[32]{0:T(128)S(1)}) all-reduce(f32[32,108]{1,0:T(8,128)S(1)} %fusion.11, f32[32]{0:T(128)S(1)} %reduce_sum.12), channel_id=2, replica_groups=mesh['gx'=8,'gy'=4] {'gy'}, use_global_device_ids=true, to_apply=%region_0.1.clone | all-reduce | flops 3488 | bytes 27904
  140.1 20.3 %all-reduce.5 = (f32[8,108]{1,0:T(8,128)}, f32[8]{0:T(128)}) all-reduce(f32[8,108]{1,0:T(8,128)S(1)} %constant_dynamic-slice_fusion, f32[8]{0:T(128)S(1)} %dynamic-slice.3), channel_id=1, replica_groups=mesh['gx'=8,'gy'=4] {'gx'}, use_global_device_ids=true, to_apply=%region_1.2 | all-reduce | flops 872 | bytes 6976 | tf_op jit(solution)/shard_map/psum | solution.py:78
  (83 shorter events, 28.6 us)
Async XLA Ops:
  0.6 96.7 %copy-start = (bf16[32,108]{1,0:T(8,128)(2,1)S(1)}, bf16[32,108]{1,0:T(8,128)(2,1)}, u32[]{:S(2)}) copy-start(bf16[32,108]{1,0:T(8,128)(2,1)} %param.9) | copy-start | bytes 20740
  1.5 14.7 %collective-permute-start = (bf16[4,32,256]{2,1,0:T(8,128)(2,1)S(1)}, bf16[4,32,256]{2,1,0:T(8,128)(2,1)S(1)}, u32[]{:S(2)}, u32[]{:S(2)}) collective-permute-start(bf16[4,32,256]{2,1,0:T(8,128)(2,1)S(1)} %slice_bitcast_fusion), channel_id=1, source_target_pairs={{0,4},{4,8},{8,12},{12,16},{16,20},{20,24},{24,28},{1,5},{5,9},{9,... | collective-permute-start | bytes 196616 | tf_op jit(solution)/shard_map/ppermute | solution.py:10
  17.4 2.3 %collective-permute-start.1 = (bf16[4,9,256]{2,0,1:T(4,128)(2,1)S(1)}, bf16[4,9,256]{2,0,1:T(4,128)(2,1)S(1)}, u32[]{:S(2)}, u32[]{:S(2)}) collective-permute-start(bf16[4,9,256]{2,0,1:T(4,128)(2,1)S(1)} %bitcast.116), channel_id=1, source_target_pairs={{0,1},{1,2},{2,3},{4,5},{5,6},{6,7},{8,9},{9,10},{10,11},{12,13},{... | collective-permute-start | bytes 55304 | tf_op jit(solution)/shard_map/ppermute | solution.py:10
  94.6 2.7 %copy-start.2 = (f32[32]{0:T(128)S(1)}, f32[32]{0:T(128)}, u32[]{:S(2)}) copy-start(f32[32]{0:T(128)} %param.10) | copy-start | bytes 388
  97.9 15.7 %copy-start.1 = (bf16[8,4,64,128]{3,2,1,0:T(8,128)(2,1)S(1)}, bf16[8,4,64,128]{3,2,1,0:T(8,128)(2,1)}, u32[]{:S(2)}) copy-start(bf16[8,4,64,128]{3,2,1,0:T(8,128)(2,1)} %param.11) | copy-start | bytes 1572868
  98.9 14.4 %all-to-all-start = ((bf16[32,4,16,128]{3,2,1,0:T(8,128)(2,1)}), bf16[32,4,16,128]{3,2,1,0:T(8,128)(2,1)S(1)}, u32[]{:S(2)}, u32[]{:S(2)}) async-start(bf16[32,4,16,128]{3,2,1,0:T(8,128)(2,1)} %select_convert_fusion), calls=%async_computation | async-start | bytes 1048576 | tf_op jit(solution)/shard_map/all_to_all | solution.py:60
  113.6 5.9 %copy-start.3 = (u32[32]{0:T(128)S(1)}, u32[32]{0:T(128)}, u32[]{:S(2)}) copy-start(u32[32]{0:T(128)} %constant.68) | copy-start | bytes 388
  116.0 12.3 %all-to-all-start.1 = ((bf16[8,4,64,128]{3,0,1,2:T(8,128)(2,1)}), bf16[8,4,64,128]{3,0,1,2:T(8,128)(2,1)S(1)}, u32[]{:S(2)}, u32[]{:S(2)}) async-start(bf16[8,4,64,128]{3,0,1,2:T(8,128)(2,1)} %get-tuple-element.13), calls=%async_computation.1 | async-start | bytes 1048576 | tf_op jit(solution)/shard_map/all_to_all | solution.py:68
where the time goes:
time: 161 us; the launch traced here: 160 us
  local copies, waits for them, and re-layouts  82.8 us (51%)
  blocking collectives  30.6 us (19%)
  waiting for transfers between devices  15.9 us (10%)
  starting transfers between devices  15.4 us (10%)
  between operations  8.42 us (5%)
  other arithmetic  6.2 us (4%)
    slice x37, local copies, waits for them, and re-layouts, taps(): piece = lax.slice_in_dim(piece, offset, offset + 2 * half - 1, 2, axis_no)  72.1 us
    psum x1, blocking collectives, local(): weight_grad, bias_grad = lax.psum((weight_part, bias_part), 'gx')  20.3 us
    unnamed x1, blocking collectives  10.3 us
    all_to_all x1, waiting for transfers between devices, local(): lax.all_to_all(pre_local, 'gy', split_axis=0, concat_axis=2, tiled=True)  8.57 us
    all_to_all x1, waiting for transfers between devices, local(): lax.all_to_all(grad_pre, 'gy', split_axis=2, concat_axis=0, tiled=True)  6.53 us
    ppermute x2, starting transfers between devices, from_behind(): return lax.ppermute(block, axis, route)  6.32 us
    all_to_all x1, starting transfers between devices, local(): lax.all_to_all(pre_local, 'gy', split_axis=0, concat_axis=2, tiled=True)  5.58 us
    all_to_all x1, starting transfers between devices, local(): lax.all_to_all(grad_pre, 'gy', split_axis=2, concat_axis=0, tiled=True)  3.47 us
  transfers between devices with their start and end apart: 4, of which 3 were waited for; matrix products, arithmetic and copies ran while one was open for 3% of the time, Pallas kernels for 0%

commit v1 on v0

--- a/solution.py
+++ b/solution.py
@@ -2,6 +2,18 @@
 import jax.numpy as jnp
 from jax import lax
 from jax.sharding import PartitionSpec as P
+
+
+def cut_along(x, dim, devices):
+    lengths = x.shape
+    tiles = x.reshape(*lengths[:dim], devices, lengths[dim] // devices, *lengths[dim + 1 :])
+    return jnp.moveaxis(tiles, dim, 0)
+
+
+def laid_out(pieces, dim):
+    pieces = jnp.moveaxis(pieces, 0, dim)
+    lengths = pieces.shape
+    return pieces.reshape(*lengths[:dim], lengths[dim] * lengths[dim + 1], *lengths[dim + 2 :])
 
 
 def from_behind(block, axis, distance):
@@ -65,7 +77,17 @@
     wide_live = row_ok.reshape(1, half_x, 1, 1) & wide_cols.reshape(1, 1, tiles_y * half_y, 1)
     slope = sigma * (1.0 + pre_wide * (1.0 - sigma))
     grad_pre = jnp.where(wide_live, grad_out.astype(jnp.float32) * slope, 0.0).astype(jnp.bfloat16)
-    returned = lax.all_to_all(grad_pre, "gy", split_axis=2, concat_axis=0, tiled=True)
+    devices_2, position = (lax.axis_size("gy"), lax.axis_index("gy"))
+    parts = cut_along(grad_pre, 2, devices_2)
+    whole = parts
+    for lap in range(1, devices_2):
+        target, source = ((position + lap) % devices_2, (position - lap) % devices_2)
+        sent = lax.dynamic_index_in_dim(parts, target, 0)
+        partner_block = lax.ppermute(
+            sent, "gy", [(i_2, (i_2 + lap) % devices_2) for i_2 in range(devices_2)]
+        )
+        whole = lax.dynamic_update_slice_in_dim(whole, partner_block, source, axis=0)
+    returned = laid_out(whole, 0)
     flat = returned.reshape(out_chans, -1)
     weight_full = lax.dot_general(
         flat, patches, (((1,), (1,)), ((), ())), preferred_element_type=jnp.float32

time: 161 us -> 156 us (0.969)
  waiting for transfers between devices: 15.9 us -> 12.6 us
  blocking collectives: 30.6 us -> 32.3 us
    all_to_all x1 -> x0, waiting for transfers between devices: 6.53 us -> none  [local(): lax.all_to_all(grad_pre, 'gy', split_axis=2, concat_axis=0, tiled=True)]
    all_to_all x1 -> x0, starting transfers between devices: 3.47 us -> none  [local(): lax.all_to_all(grad_pre, 'gy', split_axis=2, concat_axis=0, tiled=True)]
    ppermute x0 -> x3, waiting for transfers between devices: none -> 3.26 us  [local(): lax.ppermute(sent, 'gy', [(i_2, (i_2 + lap) % devices_2) for i_2 in range...]
    ppermute x0 -> x3, starting transfers between devices: none -> 1.96 us  [local(): lax.ppermute(sent, 'gy', [(i_2, (i_2 + lap) % devices_2) for i_2 in range...]
    unnamed x1, blocking collectives: 10.3 us -> 12 us
  transfers between devices with their start and end apart: 4 -> 6, of which waited for: 3 -> 4; matrix products, arithmetic and copies ran while one was open for 3% -> 3% of each run, Pallas kernels for 0% -> 0%
where the time goes in v1:
time: 156 us; the launch traced here: 155 us
  local copies, waits for them, and re-layouts  81.6 us (52%)
  blocking collectives  32.3 us (21%)
  starting transfers between devices  13.9 us (9%)
  waiting for transfers between devices  12.6 us (8%)
  between operations  8.47 us (5%)
  other arithmetic  5.12 us (3%)
    slice x37, local copies, waits for them, and re-layouts, taps(): piece = lax.slice_in_dim(piece, offset, offset + 2 * half - 1, 2, axis_no)  72.1 us
    psum x1, blocking collectives, local(): weight_grad, bias_grad = lax.psum((weight_part, bias_part), 'gx')  20.3 us
    unnamed x1, blocking collectives  12 us
    all_to_all x1, waiting for transfers between devices, local(): lax.all_to_all(pre_local, 'gy', split_axis=0, concat_axis=2, tiled=True)  8.57 us
    ppermute x2, starting transfers between devices, from_behind(): return lax.ppermute(block, axis, route)  6.32 us
    all_to_all x1, starting transfers between devices, local(): lax.all_to_all(pre_local, 'gy', split_axis=0, concat_axis=2, tiled=True)  5.58 us
    ppermute x3, waiting for transfers between devices, local(): lax.ppermute(sent, 'gy', [(i_2, (i_2 + lap) % devices_2) for i_2 in range...  3.26 us
  transfers between devices with their start and end apart: 6, of which 4 were waited for; matrix products, arithmetic and copies ran while one was open for 3% of the time, Pallas kernels for 0%

profile of v1, /device:TPU:0, one launch (start us, length us, event | category | flops | bytes accessed | tf_op | source)
XLA Modules:
  0.0 155.1 jit_solution(14247870315032474354)
XLA Ops:
  1.5 4.9 %collective-permute-start = (bf16[4,32,256]{2,1,0:T(8,128)(2,1)S(1)}, bf16[4,32,256]{2,1,0:T(8,128)(2,1)S(1)}, u32[]{:S(2)}, u32[]{:S(2)}) collective-permute-start(bf16[4,32,256]{2,1,0:T(8,128)(2,1)S(1)} %slice_bitcast_fusion), channel_id=1, source_target_pairs={{0,4},{4,8},{8,12},{12,16},{16,20},{20,24},{24,28},{1,5},{5,9},{9,... | collective-permute-start | bytes 196616 | tf_op jit(solution)/shard_map/ppermute | solution.py:22
  21.1 2.5 %slice.205 = bf16[4,4,16,128]{3,2,1,0:T(8,128)(2,1)S(1)} slice(bf16[4,4,16,257]{3,2,1,0:T(8,128)(2,1)S(1)} %slice.202), slice={[0:4:1], [0:4:1], [0:16:1], [2:257:2]} | slice | bytes 131072 | tf_op jit(solution)/shard_map/slice | solution.py:44
  23.7 2.5 %slice.204 = bf16[4,4,16,128]{3,2,1,0:T(8,128)(2,1)S(1)} slice(bf16[4,4,16,257]{3,2,1,0:T(8,128)(2,1)S(1)} %slice.202), slice={[0:4:1], [0:4:1], [0:16:1], [1:256:2]} | slice | bytes 131072 | tf_op jit(solution)/shard_map/slice | solution.py:44
  26.2 2.5 %slice.203 = bf16[4,4,16,128]{3,2,1,0:T(8,128)(2,1)S(1)} slice(bf16[4,4,16,257]{3,2,1,0:T(8,128)(2,1)S(1)} %slice.202), slice={[0:4:1], [0:4:1], [0:16:1], [0:255:2]} | slice | bytes 131072 | tf_op jit(solution)/shard_map/slice | solution.py:44
  29.4 2.5 %slice.197 = bf16[4,4,16,128]{3,2,1,0:T(8,128)(2,1)S(1)} slice(bf16[4,4,16,257]{3,2,1,0:T(8,128)(2,1)S(1)} %slice.194), slice={[0:4:1], [0:4:1], [0:16:1], [2:257:2]} | slice | bytes 131072 | tf_op jit(solution)/shard_map/slice | solution.py:44
  31.9 2.5 %slice.196 = bf16[4,4,16,128]{3,2,1,0:T(8,128)(2,1)S(1)} slice(bf16[4,4,16,257]{3,2,1,0:T(8,128)(2,1)S(1)} %slice.194), slice={[0:4:1], [0:4:1], [0:16:1], [1:256:2]} | slice | bytes 131072 | tf_op jit(solution)/shard_map/slice | solution.py:44
  34.5 2.5 %slice.195 = bf16[4,4,16,128]{3,2,1,0:T(8,128)(2,1)S(1)} slice(bf16[4,4,16,257]{3,2,1,0:T(8,128)(2,1)S(1)} %slice.194), slice={[0:4:1], [0:4:1], [0:16:1], [0:255:2]} | slice | bytes 131072 | tf_op jit(solution)/shard_map/slice | solution.py:44
  37.0 2.5 %slice.201 = bf16[4,4,16,128]{3,2,1,0:T(8,128)(2,1)S(1)} slice(bf16[4,4,16,257]{3,2,1,0:T(8,128)(2,1)S(1)} %slice.198), slice={[0:4:1], [0:4:1], [0:16:1], [2:257:2]} | slice | bytes 131072 | tf_op jit(solution)/shard_map/slice | solution.py:44
  39.6 2.5 %slice.200 = bf16[4,4,16,128]{3,2,1,0:T(8,128)(2,1)S(1)} slice(bf16[4,4,16,257]{3,2,1,0:T(8,128)(2,1)S(1)} %slice.198), slice={[0:4:1], [0:4:1], [0:16:1], [1:256:2]} | slice | bytes 131072 | tf_op jit(solution)/shard_map/slice | solution.py:44
  42.1 2.5 %slice.199 = bf16[4,4,16,128]{3,2,1,0:T(8,128)(2,1)S(1)} slice(bf16[4,4,16,257]{3,2,1,0:T(8,128)(2,1)S(1)} %slice.198), slice={[0:4:1], [0:4:1], [0:16:1], [0:255:2]} | slice | bytes 131072 | tf_op jit(solution)/shard_map/slice | solution.py:44
  45.0 2.5 %slice.192 = bf16[4,4,16,128]{3,2,1,0:T(8,128)(2,1)S(1)} slice(bf16[4,4,16,257]{3,2,1,0:T(8,128)(2,1)S(1)} %slice.189), slice={[0:4:1], [0:4:1], [0:16:1], [2:257:2]} | slice | bytes 131072 | tf_op jit(solution)/shard_map/slice | solution.py:44
  47.5 2.5 %slice.191 = bf16[4,4,16,128]{3,2,1,0:T(8,128)(2,1)S(1)} slice(bf16[4,4,16,257]{3,2,1,0:T(8,128)(2,1)S(1)} %slice.189), slice={[0:4:1], [0:4:1], [0:16:1], [1:256:2]} | slice | bytes 131072 | tf_op jit(solution)/shard_map/slice | solution.py:44
  50.1 2.5 %slice.190 = bf16[4,4,16,128]{3,2,1,0:T(8,128)(2,1)S(1)} slice(bf16[4,4,16,257]{3,2,1,0:T(8,128)(2,1)S(1)} %slice.189), slice={[0:4:1], [0:4:1], [0:16:1], [0:255:2]} | slice | bytes 131072 | tf_op jit(solution)/shard_map/slice | solution.py:44
  53.2 2.5 %slice.184 = bf16[4,4,16,128]{3,2,1,0:T(8,128)(2,1)S(1)} slice(bf16[4,4,16,257]{3,2,1,0:T(8,128)(2,1)S(1)} %slice.181), slice={[0:4:1], [0:4:1], [0:16:1], [2:257:2]} | slice | bytes 131072 | tf_op jit(solution)/shard_map/slice | solution.py:44
  55.8 2.5 %slice.183 = bf16[4,4,16,128]{3,2,1,0:T(8,128)(2,1)S(1)} slice(bf16[4,4,16,257]{3,2,1,0:T(8,128)(2,1)S(1)} %slice.181), slice={[0:4:1], [0:4:1], [0:16:1], [1:256:2]} | slice | bytes 131072 | tf_op jit(solution)/shard_map/slice | solution.py:44
  58.3 2.5 %slice.182 = bf16[4,4,16,128]{3,2,1,0:T(8,128)(2,1)S(1)} slice(bf16[4,4,16,257]{3,2,1,0:T(8,128)(2,1)S(1)} %slice.181), slice={[0:4:1], [0:4:1], [0:16:1], [0:255:2]} | slice | bytes 131072 | tf_op jit(solution)/shard_map/slice | solution.py:44
  60.9 2.5 %slice.188 = bf16[4,4,16,128]{3,2,1,0:T(8,128)(2,1)S(1)} slice(bf16[4,4,16,257]{3,2,1,0:T(8,128)(2,1)S(1)} %slice.185), slice={[0:4:1], [0:4:1], [0:16:1], [2:257:2]} | slice | bytes 131072 | tf_op jit(solution)/shard_map/slice | solution.py:44
  63.4 2.5 %slice.187 = bf16[4,4,16,128]{3,2,1,0:T(8,128)(2,1)S(1)} slice(bf16[4,4,16,257]{3,2,1,0:T(8,128)(2,1)S(1)} %slice.185), slice={[0:4:1], [0:4:1], [0:16:1], [1:256:2]} | slice | bytes 131072 | tf_op jit(solution)/shard_map/slice | solution.py:44
  66.0 2.5 %slice.186 = bf16[4,4,16,128]{3,2,1,0:T(8,128)(2,1)S(1)} slice(bf16[4,4,16,257]{3,2,1,0:T(8,128)(2,1)S(1)} %slice.185), slice={[0:4:1], [0:4:1], [0:16:1], [0:255:2]} | slice | bytes 131072 | tf_op jit(solution)/shard_map/slice | solution.py:44
  68.9 2.5 %slice.179 = bf16[4,4,16,128]{3,2,1,0:T(8,128)(2,1)S(1)} slice(bf16[4,4,16,257]{3,2,1,0:T(8,128)(2,1)S(1)} %slice.176), slice={[0:4:1], [0:4:1], [0:16:1], [2:257:2]} | slice | bytes 131072 | tf_op jit(solution)/shard_map/slice | solution.py:44
  71.4 2.5 %slice.178 = bf16[4,4,16,128]{3,2,1,0:T(8,128)(2,1)S(1)} slice(bf16[4,4,16,257]{3,2,1,0:T(8,128)(2,1)S(1)} %slice.176), slice={[0:4:1], [0:4:1], [0:16:1], [1:256:2]} | slice | bytes 131072 | tf_op jit(solution)/shard_map/slice | solution.py:44
  74.0 2.5 %slice.177 = bf16[4,4,16,128]{3,2,1,0:T(8,128)(2,1)S(1)} slice(bf16[4,4,16,257]{3,2,1,0:T(8,128)(2,1)S(1)} %slice.176), slice={[0:4:1], [0:4:1], [0:16:1], [0:255:2]} | slice | bytes 131072 | tf_op jit(solution)/shard_map/slice | solution.py:44
  77.1 2.7 %slice.171 = bf16[4,4,16,128]{3,2,1,0:T(8,128)(2,1)S(1)} slice(bf16[4,4,16,257]{3,2,1,0:T(8,128)(2,1)S(1)} %slice.168), slice={[0:4:1], [0:4:1], [0:16:1], [2:257:2]} | slice | bytes 131072 | tf_op jit(solution)/shard_map/slice | solution.py:44
  79.8 2.5 %slice.170 = bf16[4,4,16,128]{3,2,1,0:T(8,128)(2,1)S(1)} slice(bf16[4,4,16,257]{3,2,1,0:T(8,128)(2,1)S(1)} %slice.168), slice={[0:4:1], [0:4:1], [0:16:1], [1:256:2]} | slice | bytes 131072 | tf_op jit(solution)/shard_map/slice | solution.py:44
  82.4 2.5 %slice.169 = bf16[4,4,16,128]{3,2,1,0:T(8,128)(2,1)S(1)} slice(bf16[4,4,16,257]{3,2,1,0:T(8,128)(2,1)S(1)} %slice.168), slice={[0:4:1], [0:4:1], [0:16:1], [0:255:2]} | slice | bytes 131072 | tf_op jit(solution)/shard_map/slice | solution.py:44
  84.9 2.5 %slice.175 = bf16[4,4,16,128]{3,2,1,0:T(8,128)(2,1)S(1)} slice(bf16[4,4,16,257]{3,2,1,0:T(8,128)(2,1)S(1)} %slice.172), slice={[0:4:1], [0:4:1], [0:16:1], [2:257:2]} | slice | bytes 131072 | tf_op jit(solution)/shard_map/slice | solution.py:44
  87.5 2.5 %slice.174 = bf16[4,4,16,128]{3,2,1,0:T(8,128)(2,1)S(1)} slice(bf16[4,4,16,257]{3,2,1,0:T(8,128)(2,1)S(1)} %slice.172), slice={[0:4:1], [0:4:1], [0:16:1], [1:256:2]} | slice | bytes 131072 | tf_op jit(solution)/shard_map/slice | solution.py:44
  94.6 2.7 %reshape.146 = bf16[108,8192]{1,0:T(8,128)(2,1)S(1)} reshape(bf16[4,27,4,16,128]{4,3,2,1,0:T(8,128)(2,1)} %copy.17) | data formatting | bytes 3538944 | tf_op jit(solution)/shard_map/reshape | solution.py:64
  98.9 5.6 %all-to-all-start = ((bf16[32,4,16,128]{3,2,1,0:T(8,128)(2,1)}), bf16[32,4,16,128]{3,2,1,0:T(8,128)(2,1)S(1)}, u32[]{:S(2)}, u32[]{:S(2)}) async-start(bf16[32,4,16,128]{3,2,1,0:T(8,128)(2,1)} %select_convert_fusion), calls=%async_computation | async-start | bytes 1048576 | tf_op jit(solution)/shard_map/all_to_all | solution.py:72
  104.7 8.6 %all-to-all-done = bf16[32,4,16,128]{3,2,1,0:T(8,128)(2,1)S(1)} async-done(((bf16[32,4,16,128]{3,2,1,0:T(8,128)(2,1)}), bf16[32,4,16,128]{3,2,1,0:T(8,128)(2,1)S(1)}, u32[]{:S(2)}, u32[]{:S(2)}) %all-to-all-start) | async-done | bytes 524320 | tf_op jit(solution)/shard_map/all_to_all | solution.py:72
  122.7 12.0 %all-reduce.6 = (f32[32,108]{1,0:T(8,128)S(1)}, f32[32]{0:T(128)S(1)}) all-reduce(f32[32,108]{1,0:T(8,128)S(1)} %fusion.11, f32[32]{0:T(128)S(1)} %reduce_sum.12), channel_id=2, replica_groups=mesh['gx'=8,'gy'=4] {'gy'}, use_global_device_ids=true, to_apply=%region_0.1.clone | all-reduce | flops 3488 | bytes 27904
  134.7 20.3 %all-reduce.5 = (f32[8,108]{1,0:T(8,128)}, f32[8]{0:T(128)}) all-reduce(f32[8,108]{1,0:T(8,128)S(1)} %constant_dynamic-slice_fusion, f32[8]{0:T(128)S(1)} %dynamic-slice.15), channel_id=1, replica_groups=mesh['gx'=8,'gy'=4] {'gx'}, use_global_device_ids=true, to_apply=%region_1.2 | all-reduce | flops 872 | bytes 6976 | tf_op jit(solution)/shard_map/psum | solution.py:100
  (90 shorter events, 26.4 us)
Async XLA Ops:
  0.6 96.7 %copy-start = (bf16[32,108]{1,0:T(8,128)(2,1)S(1)}, bf16[32,108]{1,0:T(8,128)(2,1)}, u32[]{:S(2)}) copy-start(bf16[32,108]{1,0:T(8,128)(2,1)} %param.9) | copy-start | bytes 20740
  1.5 14.7 %collective-permute-start = (bf16[4,32,256]{2,1,0:T(8,128)(2,1)S(1)}, bf16[4,32,256]{2,1,0:T(8,128)(2,1)S(1)}, u32[]{:S(2)}, u32[]{:S(2)}) collective-permute-start(bf16[4,32,256]{2,1,0:T(8,128)(2,1)S(1)} %slice_bitcast_fusion), channel_id=1, source_target_pairs={{0,4},{4,8},{8,12},{12,16},{16,20},{20,24},{24,28},{1,5},{5,9},{9,... | collective-permute-start | bytes 196616 | tf_op jit(solution)/shard_map/ppermute | solution.py:22
  17.4 2.3 %collective-permute-start.1 = (bf16[4,9,256]{2,0,1:T(4,128)(2,1)S(1)}, bf16[4,9,256]{2,0,1:T(4,128)(2,1)S(1)}, u32[]{:S(2)}, u32[]{:S(2)}) collective-permute-start(bf16[4,9,256]{2,0,1:T(4,128)(2,1)S(1)} %bitcast.120), channel_id=1, source_target_pairs={{0,1},{1,2},{2,3},{4,5},{5,6},{6,7},{8,9},{9,10},{10,11},{12,13},{... | collective-permute-start | bytes 55304 | tf_op jit(solution)/shard_map/ppermute | solution.py:22
  94.6 2.7 %copy-start.2 = (f32[32]{0:T(128)S(1)}, f32[32]{0:T(128)}, u32[]{:S(2)}) copy-start(f32[32]{0:T(128)} %param.10) | copy-start | bytes 388
  97.9 15.5 %copy-start.1 = (bf16[8,4,64,128]{3,2,1,0:T(8,128)(2,1)S(1)}, bf16[8,4,64,128]{3,2,1,0:T(8,128)(2,1)}, u32[]{:S(2)}) copy-start(bf16[8,4,64,128]{3,2,1,0:T(8,128)(2,1)} %param.11) | copy-start | bytes 1572868
  98.9 14.4 %all-to-all-start = ((bf16[32,4,16,128]{3,2,1,0:T(8,128)(2,1)}), bf16[32,4,16,128]{3,2,1,0:T(8,128)(2,1)S(1)}, u32[]{:S(2)}, u32[]{:S(2)}) async-start(bf16[32,4,16,128]{3,2,1,0:T(8,128)(2,1)} %select_convert_fusion), calls=%async_computation | async-start | bytes 1048576 | tf_op jit(solution)/shard_map/all_to_all | solution.py:72
  113.4 1.9 %copy-start.3 = (u32[32]{0:T(128)S(1)}, u32[32]{0:T(128)}, u32[]{:S(2)}) copy-start(u32[32]{0:T(128)} %constant.114) | copy-start | bytes 388
  114.8 5.2 %collective-permute-start.2 = (bf16[1,8,4,16,128]{4,3,2,1,0:T(8,128)(2,1)S(1)}, bf16[1,8,4,16,128]{4,3,2,1,0:T(8,128)(2,1)S(1)}, u32[]{:S(2)}, u32[]{:S(2)}) collective-permute-start(bf16[1,8,4,16,128]{4,3,2,1,0:T(8,128)(2,1)S(1)} %get-tuple-element.14), channel_id=1, source_target_pairs={{0,1},{1,2},{2,3},{3,0},{4,5},{5,6},{6,7},{7,4},{8,9},{9,10},{10,1... | collective-permute-start | bytes 393224 | tf_op jit(solution)/shard_map/ppermute | solution.py:86
  114.9 6.4 %collective-permute-start.3 = (bf16[1,8,4,16,128]{4,3,2,1,0:T(8,128)(2,1)S(1)}, bf16[1,8,4,16,128]{4,3,2,1,0:T(8,128)(2,1)S(1)}, u32[]{:S(2)}, u32[]{:S(2)}) collective-permute-start(bf16[1,8,4,16,128]{4,3,2,1,0:T(8,128)(2,1)S(1)} %get-tuple-element.13), channel_id=1, source_target_pairs={{0,2},{1,3},{2,0},{3,1},{4,6},{5,7},{6,4},{7,5},{8,10},{9,11},{10,... | collective-permute-start | bytes 393224 | tf_op jit(solution)/shard_map/ppermute | solution.py:86
  116.7 4.7 %collective-permute-start.4 = (bf16[1,8,4,16,128]{4,3,2,1,0:T(8,128)(2,1)S(1)}, bf16[1,8,4,16,128]{4,3,2,1,0:T(8,128)(2,1)S(1)}, u32[]{:S(2)}, u32[]{:S(2)}) collective-permute-start(bf16[1,8,4,16,128]{4,3,2,1,0:T(8,128)(2,1)S(1)} %get-tuple-element.12), channel_id=1, source_target_pairs={{0,3},{1,0},{2,1},{3,2},{4,7},{5,4},{6,5},{7,6},{8,11},{9,8},{10,9... | collective-permute-start | bytes 393224 | tf_op jit(solution)/shard_map/ppermute | solution.py:86
